TPU v7x, 256 devices: a whole 4x4x8 slice. The times are simulated.
256 devices in a mesh: lat: 8 (over y, z_lo), lon: 8 (over x, core), dp: 4 (over z_hi).
Axes of the slice: x: 4, y: 4, z: 8 (z_hi: 4, z_lo: 2; z = z_hi * 2 + z_lo), core: 2. Of those that a mesh axis runs over, the one named last changes fastest.
Arguments:
- state_grid: bfloat16 [4, 384, 768, 128], P('dp', ('lat', 'lon')), may hold values from -6 to 6
- cotangent: bfloat16 [4, 384, 768, 128], P('dp', ('lat', 'lon')), may hold values from -6 to 6
- legendre: bfloat16 [384, 384, 384], P(('lat', 'lon')), may hold values from -0.3125 to 0.3125
- wave_ids: int32 [384], replicated, may hold values from 0 to 383, each once
- weights: bfloat16 [384, 2, 4, 1024], P('lat'), may hold values from -0.75 to 0.75
Outputs:
- input_grad: bfloat16 [4, 384, 768, 128], P('dp', ('lat', 'lon'))
- weight_grad: float32 [384, 2, 4, 1024], P('lat')
Inputs may be any that keep to these rules, and one draw needn't show every extreme that they name: wave_ids[j] is the wavenumber of slot j; each of 0 to 383 stands in exactly one slot.
All inputs are finite; a program needn't handle non-finite values.
Results may differ from a plain program's by a relative error of at most 0.034.
Values may be sent and summed in bfloat16 or wider, within the bound.
No kernel may reach another device: no remote copies, remote signals or barrier semaphores. Data moves between devices by JAX's collectives and lax.ppermute only.
A program may use at most 128 MiB of HBM per device.

v0:
```python
import math
import jax
import jax.numpy as jnp
from jax import lax
from jax.sharding import PartitionSpec as P

NLON = 768
GROUPS = 4
GROUP_WIDTH = 32


def build_tables(wave_ids):
    columns = jnp.arange(NLON, dtype=jnp.int32)
    phase_int = wave_ids[:, None] * columns[None, :] % NLON
    angles = phase_int.astype(jnp.float32) * jnp.float32(2.0 * math.pi / NLON)
    factor = jnp.float32(1.0 / math.sqrt(NLON))
    paired = jnp.stack([jnp.cos(angles) * factor, -jnp.sin(angles) * factor], axis=1)
    forward_table = paired.reshape(2 * wave_ids.shape[0], NLON)
    doubling = jnp.where(wave_ids == 0, 1.0, 2.0).astype(jnp.float32)
    inverse_table = forward_table * jnp.repeat(doubling, 2)[:, None]
    return (forward_table.astype(jnp.bfloat16), inverse_table.astype(jnp.bfloat16))


def build_kernel(weights):
    degree_count = weights.shape[0]
    real_part = weights[:, 0].reshape(degree_count, GROUPS, GROUP_WIDTH, GROUP_WIDTH)
    imag_part = weights[:, 1].reshape(degree_count, GROUPS, GROUP_WIDTH, GROUP_WIDTH)
    upper_rows = jnp.stack([real_part, imag_part], axis=3)
    lower_rows = jnp.stack([-imag_part, real_part], axis=3)
    return jnp.stack([upper_rows, lower_rows], axis=2)


def gelu_slope(branch):
    normal_cdf = 0.5 * (1.0 + lax.erf(branch * (1.0 / math.sqrt(2.0))))
    density = jnp.exp(-0.5 * branch * branch) * (1.0 / math.sqrt(2.0 * math.pi))
    return normal_cdf + branch * density


def shards(state_grid, cotangent, legendre, wave_ids, weights):
    lat_count = lax.axis_size("lat")
    lon_count = lax.axis_size("lon")
    samples, rows_dev, lon_cells, channels = state_grid.shape
    slot_count, lat_cells, degree_count = legendre.shape
    slot_reals = 2 * slot_count
    first_slot = (lax.axis_index("lat") * lon_count + lax.axis_index("lon")) * slot_count
    held_waves = lax.dynamic_slice_in_dim(wave_ids, first_slot, slot_count)
    degree_ids = jnp.arange(degree_count, dtype=jnp.int32)
    masked = jnp.where(
        degree_ids[None, None, :] >= held_waves[:, None, None],
        legendre,
        jnp.zeros((), legendre.dtype),
    )
    slot_order = wave_ids.reshape(lat_count, lon_count, slot_count).transpose(1, 0, 2).reshape(-1)
    forward_table, inverse_table = build_tables(slot_order)
    kernel = build_kernel(weights)

    def analyze(source, twiddle):
        spectra = jnp.einsum(
            "srnc,kn->srkc", source, twiddle, preferred_element_type=jnp.float32
        ).astype(jnp.bfloat16)
        gathered = lax.all_to_all(
            lax.all_to_all(spectra, "lon", split_axis=2, concat_axis=1, tiled=True),
            "lat",
            split_axis=2,
            concat_axis=1,
            tiled=True,
        )
        blocks = gathered.reshape(samples, lat_cells, slot_count, 2 * channels)
        spectral = jnp.einsum("samc,mal->slmc", blocks, masked, preferred_element_type=jnp.float32)
        spectral = spectral.astype(jnp.bfloat16).reshape(
            samples, degree_count, slot_reals, channels
        )
        return lax.all_to_all(spectral, "lat", split_axis=1, concat_axis=2, tiled=True)

    def synthesize(spectral, twiddle):
        joined = lax.all_to_all(spectral, "lat", split_axis=2, concat_axis=1, tiled=True)
        blocks = joined.reshape(samples, degree_count, slot_count, 2 * channels)
        spectra = jnp.einsum(
            "slmc,mal->samc", blocks, masked, preferred_element_type=jnp.float32
        ).astype(jnp.bfloat16)
        spectra = spectra.reshape(samples, lat_cells, slot_reals, channels)
        pencil = lax.all_to_all(
            lax.all_to_all(spectra, "lat", split_axis=1, concat_axis=2, tiled=True),
            "lon",
            split_axis=1,
            concat_axis=2,
            tiled=True,
        )
        return jnp.einsum("srkc,kn->srnc", pencil, twiddle, preferred_element_type=jnp.float32)

    def split_groups(spectral):
        return spectral.reshape(samples, spectral.shape[1], -1, 2, GROUPS, GROUP_WIDTH)

    coef_fwd = analyze(state_grid, forward_table)
    coef_six = split_groups(coef_fwd)
    mixed_coef = jnp.einsum(
        "slmpgi,lgpiqo->slmqgo", coef_six, kernel, preferred_element_type=jnp.float32
    ).astype(jnp.bfloat16)
    branch = synthesize(mixed_coef.reshape(coef_fwd.shape), inverse_table)
    pulled = (cotangent.astype(jnp.float32) * gelu_slope(branch)).astype(jnp.bfloat16)
    back_coef = analyze(pulled, inverse_table)
    back_six = split_groups(back_coef)
    outer_sums = jnp.einsum(
        "slmpgi,slmqgo->lgpiqo", coef_six, back_six, preferred_element_type=jnp.float32
    )
    real_grad = outer_sums[:, :, 0, :, 0, :] + outer_sums[:, :, 1, :, 1, :]
    imag_grad = outer_sums[:, :, 0, :, 1, :] - outer_sums[:, :, 1, :, 0, :]
    local_grad = jnp.stack([real_grad, imag_grad], axis=1).reshape(weights.shape)
    weight_grad = lax.psum(local_grad.astype(jnp.bfloat16), ("lon", "dp")).astype(jnp.float32)
    demixed = jnp.einsum(
        "slmqgo,lgpiqo->slmpgi", back_six, kernel, preferred_element_type=jnp.float32
    ).astype(jnp.bfloat16)
    returned = synthesize(demixed.reshape(back_coef.shape), forward_table)
    input_grad = (cotangent.astype(jnp.float32) + returned).astype(jnp.bfloat16)
    return (input_grad, weight_grad)


def solution(mesh):
    return jax.shard_map(
        shards,
        mesh=mesh,
        in_specs=(
            P("dp", ("lat", "lon"), None, None),
            P("dp", ("lat", "lon"), None, None),
            P(("lat", "lon"), None, None),
            P(),
            P("lat", None, None, None),
        ),
        out_specs=(P("dp", ("lat", "lon"), None, None), P("lat", None, None, None)),
        check_vma=False,
    )
```

profile of v0, /device:TPU:8, one launch (start us, length us, event | category | flops | bytes accessed | tf_op | source)
XLA Modules:
  0.0 725.3 jit_solution(13457028617643623277)
XLA Ops:
  8.2 4.9 cosine_multiply_fusion
  15.6 3.7 reshape.366
  22.5 25.9 %all_to_all.192 = bf16[1,6,768,128]{3,1,0,2:T(8,128)(2,1)S(1)} all-to-all(bf16[1,6,768,128]{3,1,0,2:T(8,128)(2,1)S(1)} %copy.223), channel_id=1, replica_groups=mesh['lat'=8,'lon'=8,'dp'=4] {'lon'}, dimensions={2} | all-to-all | bytes 2359296 | tf_op jit(solution)/shard_map/all_to_all | solution.py:62
  50.1 6.5 all-to-all-start.1
  57.4 13.8 %all-to-all-done.1 = bf16[1,48,96,128]{3,1,0,2:T(8,128)(2,1)S(1)} async-done(((bf16[1,48,96,128]{3,1,0,2:T(8,128)(2,1)}), bf16[1,48,96,128]{3,1,0,2:T(8,128)(2,1)S(1)}, u32[]{:S(2)}, u32[]{:S(2)}) %all-to-all-start.1) | async-done | bytes 1179680 | tf_op jit(solution)/shard_map/all_to_all | solution.py:61
  71.2 3.0 copy.280
  74.2 4.4 reshape.378
  78.7 3.4 convolution_convert_fusion.1
  82.1 2.9 copy.229
  85.0 6.4 all-to-all-start.2
  100.2 3.0 pad_maximum_fusion
  103.2 12.7 %copy.232 = bf16[48,4,2,32,2,32]{3,5,2,4,1,0:T(8,128)(2,1)} copy(bf16[48,4,2,32,2,32]{0,5,4,3,1,2:T(8,128)(2,1)} %pad_maximum_fusion) | data formatting | bytes 3145728 | tf_op jit(solution)/shard_map/stack | solution.py:30
  120.3 8.3 %copy.270 = bf16[48,48,2,4,32,1]{1,4,2,5,3,0:T(8,128)(2,1)} copy(bf16[48,48,2,4,32,1]{0,4,3,2,1,5:T(8,128)(2,1)} %bitcast.179) | data formatting | bytes 2359296 | tf_op jit(solution)/shard_map/reshape.8
  128.5 6.7 fusion
  135.3 8.3 %copy.234 = bf16[1,48,48,2,4,32]{1,5,4,3,2,0:T(8,128)(2,1)} copy(bf16[1,48,48,2,4,32]{2,5,3,4,1,0:T(8,128)(2,1)} %fusion) | data formatting | bytes 2359296 | tf_op jit(solution)/shard_map/convert_element_type | solution.py:98
  143.5 3.2 copy.235
  146.7 19.4 %all_to_all.193 = bf16[1,48,96,128]{3,1,0,2:T(8,128)(2,1)} all-to-all(bf16[1,48,96,128]{3,1,0,2:T(8,128)(2,1)S(1)} %copy.235), channel_id=1, replica_groups=mesh['lat'=8,'lon'=8,'dp'=4] {'lat'}, dimensions={2} | all-to-all | bytes 2359296 | tf_op jit(solution)/shard_map/all_to_all | solution.py:76
  166.2 4.2 copy.283
  170.4 4.4 reshape.379
  174.8 3.5 convolution_convert_fusion.3
  178.3 2.9 copy.238
  181.2 21.5 %all_to_all.194 = bf16[1,384,12,128]{3,2,0,1:T(8,128)(2,1)S(1)} all-to-all(bf16[1,384,12,128]{3,2,0,1:T(8,128)(2,1)} %copy.238), channel_id=1, replica_groups=mesh['lat'=8,'lon'=8,'dp'=4] {'lat'}, dimensions={1} | all-to-all | bytes 2359296 | tf_op jit(solution)/shard_map/all_to_all | solution.py:83
  204.4 4.3 all-to-all-start.5
  211.1 14.9 %all-to-all-done.5 = bf16[1,48,96,128]{3,2,0,1:T(8,128)(2,1)} async-done(((bf16[1,48,96,128]{3,2,0,1:T(8,128)(2,1)}), bf16[1,48,96,128]{3,2,0,1:T(8,128)(2,1)}, u32[]{:S(2)}, u32[]{:S(2)}) %all-to-all-start.5) | async-done | bytes 1179680 | tf_op jit(solution)/shard_map/all_to_all | solution.py:82
  227.4 4.8 fusion.15
  234.4 24.2 %all_to_all.195 = bf16[1,6,768,128]{3,1,0,2:T(8,128)(2,1)S(1)} all-to-all(bf16[1,6,768,128]{3,1,0,2:T(8,128)(2,1)S(1)} %copy.244), channel_id=1, replica_groups=mesh['lat'=8,'lon'=8,'dp'=4] {'lon'}, dimensions={2} | all-to-all | bytes 2359296 | tf_op jit(solution)/shard_map/all_to_all | solution.py:62
  259.3 20.1 %all_to_all.196 = bf16[1,48,96,128]{3,1,0,2:T(8,128)(2,1)S(1)} all-to-all(bf16[1,48,96,128]{3,1,0,2:T(8,128)(2,1)S(1)} %copy.247), channel_id=1, replica_groups=mesh['lat'=8,'lon'=8,'dp'=4] {'lat'}, dimensions={2} | all-to-all | bytes 2359296 | tf_op jit(solution)/shard_map/all_to_all | solution.py:61
  279.4 3.0 copy.284
  282.4 4.4 reshape.380
  291.1 5.1 all-to-all-start.8
  296.3 11.6 %copy.253 = bf16[48,4,2,32,2,32]{5,3,4,2,1,0:T(8,128)(2,1)} copy(bf16[48,4,2,32,2,32]{0,5,4,3,1,2:T(8,128)(2,1)} %pad_maximum_fusion) | data formatting | bytes 3145728 | tf_op jit(solution)/shard_map/stack | solution.py:30
  307.8 6.3 all-to-all-done.8
  314.5 2.7 copy.252
  317.2 8.3 %copy.273 = bf16[48,48,2,4,32,1]{1,4,2,5,3,0:T(8,128)(2,1)} copy(bf16[48,48,2,4,32,1]{0,4,3,2,1,5:T(8,128)(2,1)} %bitcast.182) | data formatting | bytes 2359296 | tf_op jit(solution)/shard_map/reshape.39
  325.5 6.8 fusion.1
  332.3 8.3 %copy.255 = bf16[1,48,48,2,4,32]{1,5,4,3,2,0:T(8,128)(2,1)} copy(bf16[1,48,48,2,4,32]{2,5,3,4,1,0:T(8,128)(2,1)} %fusion.1) | data formatting | bytes 2359296 | tf_op jit(solution)/shard_map/convert_element_type | solution.py:112
  340.6 3.2 copy.256
  343.8 19.7 %all_to_all.197 = bf16[1,48,96,128]{3,1,0,2:T(8,128)(2,1)S(1)} all-to-all(bf16[1,48,96,128]{3,1,0,2:T(8,128)(2,1)S(1)} %copy.256), channel_id=1, replica_groups=mesh['lat'=8,'lon'=8,'dp'=4] {'lat'}, dimensions={2} | all-to-all | bytes 2359296 | tf_op jit(solution)/shard_map/all_to_all | solution.py:76
  363.5 3.0 copy.287
  366.4 4.4 reshape.381
  375.3 5.3 all-to-all-start.10
  380.6 8.3 %copy.276 = bf16[48,48,2,4,32,1]{1,4,5,2,3,0:T(8,128)(2,1)} copy(bf16[48,48,2,4,32,1]{0,4,3,2,1,5:T(8,128)(2,1)} %bitcast.180) | data formatting | bytes 2359296 | tf_op jit(solution)/shard_map/reshape.8
  388.9 12.5 %fusion.41 = f32[48,4,2,32,2,32]{5,3,4,2,1,0:T(8,128)} fusion(bf16[48,48,2,4,32,1]{1,4,5,2,3,0:T(8,128)(2,1)} %copy.276, bf16[48,48,2,4,32,1]{1,4,2,5,3,0:T(8,128)(2,1)} %copy.273), kind=kOutput, calls=%fused_computation.66 | convolution fusion | flops 75497472 | bytes 5505024 | tf_op jit(solution)/shard_map/slmpgi,slmqgo->lgpiqo/dot_general | solution.py:103
  403.1 4.3 all-to-all-start.11
  407.4 7.5 %fusion.3 = (bf16[48,4,1,32,1,32]{5,3,4,2,1,0:T(8,128)(2,1)}, bf16[48,4,1,32,1,32]{5,3,4,2,1,0:T(8,128)(2,1)S(1)}) fusion(f32[48,4,2,32,2,32]{5,3,4,2,1,0:T(8,128)} %fusion.41), kind=kLoop, calls=%fused_computation.9 | loop fusion | flops 786432 | bytes 3932160 | tf_op jit(solution)/shard_map/convert.3
  415.0 2.9 reshape.382
  421.6 290.0 %all-reduce.2.cloned.1.call-done = bf16[48,2,4,1024]{3,0,2,1:T(8,128)(2,1)} async-done(((bf16[48,2,4,1024]{3,0,2,1:T(8,128)(2,1)}), bf16[48,2,4,1024]{3,0,2,1:T(8,128)(2,1)}) %all-reduce.2.cloned.1.call-update) | async-done | bytes 786448 | tf_op jit(solution)/shard_map/psum | solution.py:109
  711.6 2.9 copy.269
  (62 shorter events, 48.9 us)
Async XLA Ops:
  7.2 12.2 %copy-start = (bf16[1,6,768,128]{3,2,1,0:T(8,128)(2,1)S(1)}, bf16[1,6,768,128]{3,2,1,0:T(8,128)(2,1)}, u32[]{:S(2)}) copy-start(bf16[1,6,768,128]{3,2,1,0:T(8,128)(2,1)} %param.5) | copy-start | bytes 3538948
  50.1 21.1 %all-to-all-start.1 = ((bf16[1,48,96,128]{3,1,0,2:T(8,128)(2,1)}), bf16[1,48,96,128]{3,1,0,2:T(8,128)(2,1)S(1)}, u32[]{:S(2)}, u32[]{:S(2)}) async-start(bf16[1,48,96,128]{3,1,0,2:T(8,128)(2,1)} %copy.226), calls=%async_computation.1 | async-start | bytes 2359296 | tf_op jit(solution)/shard_map/all_to_all | solution.py:61
  85.0 6.4 copy-start.3
  85.0 30.9 %all-to-all-start.2 = ((bf16[1,384,12,128]{3,2,0,1:T(8,128)(2,1)}), bf16[1,384,12,128]{3,2,0,1:T(8,128)(2,1)}, u32[]{:S(2)}, u32[]{:S(2)}) async-start(bf16[1,384,12,128]{3,2,0,1:T(8,128)(2,1)} %copy.229), calls=%async_computation.2 | async-start | bytes 3145728 | tf_op jit(solution)/shard_map/all_to_all | solution.py:73
  204.4 21.6 %all-to-all-start.5 = ((bf16[1,48,96,128]{3,2,0,1:T(8,128)(2,1)}), bf16[1,48,96,128]{3,2,0,1:T(8,128)(2,1)}, u32[]{:S(2)}, u32[]{:S(2)}) async-start(bf16[1,48,96,128]{3,2,0,1:T(8,128)(2,1)} %copy.241), calls=%async_computation.5 | async-start | bytes 2359296 | tf_op jit(solution)/shard_map/all_to_all | solution.py:82
  291.1 23.0 %all-to-all-start.8 = ((bf16[1,384,12,128]{3,2,0,1:T(8,128)(2,1)}), bf16[1,384,12,128]{3,2,0,1:T(8,128)(2,1)S(1)}, u32[]{:S(2)}, u32[]{:S(2)}) async-start(bf16[1,384,12,128]{3,2,0,1:T(8,128)(2,1)} %copy.250), calls=%async_computation.8 | async-start | bytes 3145728 | tf_op jit(solution)/shard_map/all_to_all | solution.py:73
  375.3 26.1 %all-to-all-start.10 = ((bf16[1,384,12,128]{3,2,0,1:T(8,128)(2,1)}), bf16[1,384,12,128]{3,2,0,1:T(8,128)(2,1)S(1)}, u32[]{:S(2)}, u32[]{:S(2)}) async-start(bf16[1,384,12,128]{3,2,0,1:T(8,128)(2,1)} %copy.259), calls=%async_computation.10 | async-start | bytes 3145728 | tf_op jit(solution)/shard_map/all_to_all | solution.py:83
  403.1 311.3 %all-to-all-start.11 = ((bf16[1,48,96,128]{3,2,0,1:T(8,128)(2,1)}), bf16[1,48,96,128]{3,2,0,1:T(8,128)(2,1)}, u32[]{:S(2)}, u32[]{:S(2)}) async-start(bf16[1,48,96,128]{3,2,0,1:T(8,128)(2,1)} %copy.262), calls=%async_computation.11 | async-start | bytes 2359296 | tf_op jit(solution)/shard_map/all_to_all | solution.py:82
  407.4 304.2 %all-reduce.2.cloned.1.call-start = ((), (), s32[]{:S(2)}) async-start(), calls=%async_computation.12 | async-start | bytes 1572864 | tf_op jit(solution)/shard_map/psum | solution.py:109
  419.5 1.6 copy-start.2
  714.5 1.6 copy-start.4
  716.1 2.1 copy-start.1
Sparse Core Ops, SparseCore 0:
  420.8 290.7 all-reduce.1
where the time goes:
time: 735 us; the launch traced here: 725 us
  waiting for transfers between devices  325 us (44%)
  local copies, waits for them, and re-layouts  155 us (21%)
  blocking collectives  131 us (18%)
  matrix products  47 us (6%)
  starting transfers between devices  31.8 us (4%)
  other arithmetic  20.7 us (3%)
  between operations  14.6 us (2%)
    psum x1, waiting for transfers between devices, shards(): lax.psum(local_grad.astype(jnp.bfloat16), ('lon', 'dp')).astype(jnp.float32)  290 us
    another operation x11, local copies, waits for them, and re-layouts  55.7 us
    all_to_all x2, blocking collectives, analyze(): lax.all_to_all(spectra, 'lon', split_axis=2, concat_axis=1, tiled=True)  50.1 us
    all_to_all x2, blocking collectives, synthesize(): lax.all_to_all(spectral, 'lat', split_axis=2, concat_axis=1, tiled=True)  39.1 us
    another operation x2, local copies, waits for them, and re-layouts, build_kernel(): return jnp.stack([upper_rows, lower_rows], axis=2)  24.2 us
    all_to_all x1, blocking collectives, synthesize(): lax.all_to_all(spectra, 'lat', split_axis=1, concat_axis=2, tiled=True)  21.5 us
    all_to_all x1, blocking collectives, analyze(): lax.all_to_all(lax.all_to_all(spectra, 'lon', split_axis=2, concat_axis=1...  20.1 us
    all_to_all x2, waiting for transfers between devices, synthesize(): lax.all_to_all(lax.all_to_all(spectra, 'lat', split_axis=1, concat_axis=2...  14.9 us
  transfers between devices with their start and end apart: 7, of which 4 were waited for; matrix products, arithmetic and copies ran while one was open for 11% of the time, Pallas kernels for 0%

commit v1 on v0

--- a/solution.py
+++ b/solution.py
@@ -7,6 +7,10 @@
 NLON = 768
 GROUPS = 4
 GROUP_WIDTH = 32
+
+
+def regions_lift(block_here, a_name, mesh_ax="dp"):
+    return lax.psum(lax.psum(block_here, a_name), axis_name=mesh_ax)
 
 
 def build_tables(wave_ids):
@@ -106,7 +110,7 @@
     real_grad = outer_sums[:, :, 0, :, 0, :] + outer_sums[:, :, 1, :, 1, :]
     imag_grad = outer_sums[:, :, 0, :, 1, :] - outer_sums[:, :, 1, :, 0, :]
     local_grad = jnp.stack([real_grad, imag_grad], axis=1).reshape(weights.shape)
-    weight_grad = lax.psum(local_grad.astype(jnp.bfloat16), ("lon", "dp")).astype(jnp.float32)
+    weight_grad = regions_lift(local_grad.astype(jnp.bfloat16), "lon").astype(jnp.float32)
     demixed = jnp.einsum(
         "slmqgo,lgpiqo->slmpgi", back_six, kernel, preferred_element_type=jnp.float32
     ).astype(jnp.bfloat16)

time: 735 us -> 563 us (0.77)
  waiting for transfers between devices: 325 us -> 161 us
    psum x1 -> x2, waiting for transfers between devices: 290 us -> 126 us  [regions_lift(): return lax.psum(lax.psum(block_here, a_name), axis_name=mesh_ax)]
  transfers between devices with their start and end apart: 7 -> 8, of which waited for: 4 -> 5; matrix products, arithmetic and copies ran while one was open for 11% -> 13% of each run, Pallas kernels for 0% -> 0%
where the time goes in v1:
time: 563 us; the launch traced here: 552 us
  waiting for transfers between devices  161 us (29%)
  local copies, waits for them, and re-layouts  156 us (28%)
  blocking collectives  131 us (23%)
  matrix products  42.4 us (8%)
  starting transfers between devices  31.2 us (6%)
  other arithmetic  16.4 us (3%)
  between operations  14.6 us (3%)
    psum x2, waiting for transfers between devices, regions_lift(): return lax.psum(lax.psum(block_here, a_name), axis_name=mesh_ax)  126 us
    another operation x11, local copies, waits for them, and re-layouts  55.6 us
    all_to_all x2, blocking collectives, analyze(): lax.all_to_all(spectra, 'lon', split_axis=2, concat_axis=1, tiled=True)  50.1 us
    all_to_all x2, blocking collectives, synthesize(): lax.all_to_all(spectral, 'lat', split_axis=2, concat_axis=1, tiled=True)  39.1 us
    another operation x2, local copies, waits for them, and re-layouts, build_kernel(): return jnp.stack([upper_rows, lower_rows], axis=2)  24.2 us
    all_to_all x1, blocking collectives, synthesize(): lax.all_to_all(spectra, 'lat', split_axis=1, concat_axis=2, tiled=True)  21.5 us
    all_to_all x1, blocking collectives, analyze(): lax.all_to_all(lax.all_to_all(spectra, 'lon', split_axis=2, concat_axis=1...  20.1 us
    all_to_all x2, waiting for transfers between devices, synthesize(): lax.all_to_all(lax.all_to_all(spectra, 'lat', split_axis=1, concat_axis=2...  14.9 us
  transfers between devices with their start and end apart: 8, of which 5 were waited for; matrix products, arithmetic and copies ran while one was open for 13% of the time, Pallas kernels for 0%

profile of v1, /device:TPU:8, one launch (start us, length us, event | category | flops | bytes accessed | tf_op | source)
XLA Modules:
  0.0 552.5 jit_solution(8054474275673524559)
XLA Ops:
  8.2 4.9 cosine_multiply_fusion
  15.6 3.7 reshape.366
  22.5 25.9 %all_to_all.192 = bf16[1,6,768,128]{3,1,0,2:T(8,128)(2,1)S(1)} all-to-all(bf16[1,6,768,128]{3,1,0,2:T(8,128)(2,1)S(1)} %copy.223), channel_id=1, replica_groups=mesh['lat'=8,'lon'=8,'dp'=4] {'lon'}, dimensions={2} | all-to-all | bytes 2359296 | tf_op jit(solution)/shard_map/all_to_all | solution.py:66
  50.1 6.5 %all-to-all-start.1 = ((bf16[1,48,96,128]{3,1,0,2:T(8,128)(2,1)}), bf16[1,48,96,128]{3,1,0,2:T(8,128)(2,1)S(1)}, u32[]{:S(2)}, u32[]{:S(2)}) async-start(bf16[1,48,96,128]{3,1,0,2:T(8,128)(2,1)} %copy.226), calls=%async_computation.1 | async-start | bytes 2359296 | tf_op jit(solution)/shard_map/all_to_all | solution.py:65
  57.4 13.8 %all-to-all-done.1 = bf16[1,48,96,128]{3,1,0,2:T(8,128)(2,1)S(1)} async-done(((bf16[1,48,96,128]{3,1,0,2:T(8,128)(2,1)}), bf16[1,48,96,128]{3,1,0,2:T(8,128)(2,1)S(1)}, u32[]{:S(2)}, u32[]{:S(2)}) %all-to-all-start.1) | async-done | bytes 1179680 | tf_op jit(solution)/shard_map/all_to_all | solution.py:65
  71.2 3.0 copy.280
  74.2 4.4 reshape.378
  78.7 3.4 convolution_convert_fusion.1
  82.1 2.9 copy.229
  85.0 6.4 %all-to-all-start.2 = ((bf16[1,384,12,128]{3,2,0,1:T(8,128)(2,1)}), bf16[1,384,12,128]{3,2,0,1:T(8,128)(2,1)}, u32[]{:S(2)}, u32[]{:S(2)}) async-start(bf16[1,384,12,128]{3,2,0,1:T(8,128)(2,1)} %copy.229), calls=%async_computation.2 | async-start | bytes 3145728 | tf_op jit(solution)/shard_map/all_to_all | solution.py:77
  100.2 3.0 pad_maximum_fusion
  103.2 12.7 %copy.232 = bf16[48,4,2,32,2,32]{3,5,2,4,1,0:T(8,128)(2,1)} copy(bf16[48,4,2,32,2,32]{0,5,4,3,1,2:T(8,128)(2,1)} %pad_maximum_fusion) | data formatting | bytes 3145728 | tf_op jit(solution)/shard_map/stack | solution.py:34
  120.3 8.3 %copy.270 = bf16[48,48,2,4,32,1]{1,4,2,5,3,0:T(8,128)(2,1)} copy(bf16[48,48,2,4,32,1]{0,4,3,2,1,5:T(8,128)(2,1)} %bitcast.179) | data formatting | bytes 2359296 | tf_op jit(solution)/shard_map/reshape.8
  128.5 6.7 %fusion = bf16[1,48,48,2,4,32]{2,5,3,4,1,0:T(8,128)(2,1)} fusion(bf16[48,4,2,32,2,32]{3,5,2,4,1,0:T(8,128)(2,1)} %copy.232, bf16[48,48,2,4,32,1]{1,4,2,5,3,0:T(8,128)(2,1)} %copy.270), kind=kOutput, calls=%fused_computation.4 | convolution fusion | flops 76087296 | bytes 3932160 | tf_op jit(solution)/shard_map/slmpgi,lgpiqo->slmqgo/dot_general | solution.py:100
  135.3 8.3 %copy.234 = bf16[1,48,48,2,4,32]{1,5,4,3,2,0:T(8,128)(2,1)} copy(bf16[1,48,48,2,4,32]{2,5,3,4,1,0:T(8,128)(2,1)} %fusion) | data formatting | bytes 2359296 | tf_op jit(solution)/shard_map/convert_element_type | solution.py:102
  143.5 3.2 copy.235
  146.7 19.4 %all_to_all.193 = bf16[1,48,96,128]{3,1,0,2:T(8,128)(2,1)} all-to-all(bf16[1,48,96,128]{3,1,0,2:T(8,128)(2,1)S(1)} %copy.235), channel_id=1, replica_groups=mesh['lat'=8,'lon'=8,'dp'=4] {'lat'}, dimensions={2} | all-to-all | bytes 2359296 | tf_op jit(solution)/shard_map/all_to_all | solution.py:80
  166.2 4.2 copy.283
  170.4 4.4 reshape.379
  174.8 3.5 convolution_convert_fusion.3
  178.3 2.9 copy.238
  181.2 21.5 %all_to_all.194 = bf16[1,384,12,128]{3,2,0,1:T(8,128)(2,1)S(1)} all-to-all(bf16[1,384,12,128]{3,2,0,1:T(8,128)(2,1)} %copy.238), channel_id=1, replica_groups=mesh['lat'=8,'lon'=8,'dp'=4] {'lat'}, dimensions={1} | all-to-all | bytes 2359296 | tf_op jit(solution)/shard_map/all_to_all | solution.py:87
  204.4 4.3 all-to-all-start.5
  211.1 14.9 %all-to-all-done.5 = bf16[1,48,96,128]{3,2,0,1:T(8,128)(2,1)} async-done(((bf16[1,48,96,128]{3,2,0,1:T(8,128)(2,1)}), bf16[1,48,96,128]{3,2,0,1:T(8,128)(2,1)}, u32[]{:S(2)}, u32[]{:S(2)}) %all-to-all-start.5) | async-done | bytes 1179680 | tf_op jit(solution)/shard_map/all_to_all | solution.py:86
  227.4 4.8 fusion.15
  234.4 24.2 %all_to_all.195 = bf16[1,6,768,128]{3,1,0,2:T(8,128)(2,1)S(1)} all-to-all(bf16[1,6,768,128]{3,1,0,2:T(8,128)(2,1)S(1)} %copy.244), channel_id=1, replica_groups=mesh['lat'=8,'lon'=8,'dp'=4] {'lon'}, dimensions={2} | all-to-all | bytes 2359296 | tf_op jit(solution)/shard_map/all_to_all | solution.py:66
  259.3 20.1 %all_to_all.196 = bf16[1,48,96,128]{3,1,0,2:T(8,128)(2,1)S(1)} all-to-all(bf16[1,48,96,128]{3,1,0,2:T(8,128)(2,1)S(1)} %copy.247), channel_id=1, replica_groups=mesh['lat'=8,'lon'=8,'dp'=4] {'lat'}, dimensions={2} | all-to-all | bytes 2359296 | tf_op jit(solution)/shard_map/all_to_all | solution.py:65
  279.4 3.0 copy.284
  282.4 4.4 reshape.380
  291.1 5.1 all-to-all-start.8
  296.3 11.6 %copy.253 = bf16[48,4,2,32,2,32]{5,3,4,2,1,0:T(8,128)(2,1)} copy(bf16[48,4,2,32,2,32]{0,5,4,3,1,2:T(8,128)(2,1)} %pad_maximum_fusion) | data formatting | bytes 3145728 | tf_op jit(solution)/shard_map/stack | solution.py:34
  307.8 6.3 %all-to-all-done.8 = bf16[1,384,12,128]{3,2,0,1:T(8,128)(2,1)S(1)} async-done(((bf16[1,384,12,128]{3,2,0,1:T(8,128)(2,1)}), bf16[1,384,12,128]{3,2,0,1:T(8,128)(2,1)S(1)}, u32[]{:S(2)}, u32[]{:S(2)}) %all-to-all-start.8) | async-done | bytes 1179680 | tf_op jit(solution)/shard_map/all_to_all | solution.py:77
  317.2 8.2 %copy.273 = bf16[48,48,2,4,32,1]{1,4,2,5,3,0:T(8,128)(2,1)} copy(bf16[48,48,2,4,32,1]{0,4,3,2,1,5:T(8,128)(2,1)} %bitcast.182) | data formatting | bytes 2359296 | tf_op jit(solution)/shard_map/reshape.39
  325.5 6.7 %fusion.1 = bf16[1,48,48,2,4,32]{2,5,3,4,1,0:T(8,128)(2,1)} fusion(bf16[48,4,2,32,2,32]{5,3,4,2,1,0:T(8,128)(2,1)} %copy.253, bf16[48,48,2,4,32,1]{1,4,2,5,3,0:T(8,128)(2,1)} %copy.273), kind=kOutput, calls=%fused_computation.5 | convolution fusion | flops 76087296 | bytes 3932160 | tf_op jit(solution)/shard_map/slmqgo,lgpiqo->slmpgi/dot_general | solution.py:114
  332.2 8.3 %copy.255 = bf16[1,48,48,2,4,32]{1,5,4,3,2,0:T(8,128)(2,1)} copy(bf16[1,48,48,2,4,32]{2,5,3,4,1,0:T(8,128)(2,1)} %fusion.1) | data formatting | bytes 2359296 | tf_op jit(solution)/shard_map/convert_element_type | solution.py:116
  340.4 3.2 copy.256
  343.6 19.7 %all_to_all.197 = bf16[1,48,96,128]{3,1,0,2:T(8,128)(2,1)S(1)} all-to-all(bf16[1,48,96,128]{3,1,0,2:T(8,128)(2,1)S(1)} %copy.256), channel_id=1, replica_groups=mesh['lat'=8,'lon'=8,'dp'=4] {'lat'}, dimensions={2} | all-to-all | bytes 2359296 | tf_op jit(solution)/shard_map/all_to_all | solution.py:80
  363.3 3.0 copy.287
  366.3 4.4 reshape.381
  375.2 5.1 all-to-all-start.10
  380.5 8.3 %copy.276 = bf16[48,48,2,4,32,1]{1,4,5,2,3,0:T(8,128)(2,1)} copy(bf16[48,48,2,4,32,1]{0,4,3,2,1,5:T(8,128)(2,1)} %bitcast.180) | data formatting | bytes 2359296 | tf_op jit(solution)/shard_map/reshape.8
  388.7 8.0 %fusion.41 = f32[48,4,2,32,2,32]{5,3,4,2,1,0:T(8,128)S(1)} fusion(bf16[48,48,2,4,32,1]{1,4,5,2,3,0:T(8,128)(2,1)} %copy.276, bf16[48,48,2,4,32,1]{1,4,2,5,3,0:T(8,128)(2,1)} %copy.273), kind=kOutput, calls=%fused_computation.66 | convolution fusion | flops 75497472 | bytes 5505024 | tf_op jit(solution)/shard_map/slmpgi,slmqgo->lgpiqo/dot_general | solution.py:107
  396.7 3.2 fusion.3
  402.9 2.9 reshape.383
  408.7 3.7 all-to-all-start.11
  412.4 64.9 %all-reduce.3.cloned.1.call-done = bf16[48,2,4,1024]{3,0,2,1:T(8,128)(2,1)} async-done(((bf16[48,2,4,1024]{3,0,2,1:T(8,128)(2,1)}), bf16[48,2,4,1024]{3,0,2,1:T(8,128)(2,1)}) %all-reduce.3.cloned.1.call-update) | async-done | bytes 786448 | tf_op jit(solution)/shard_map/psum | solution.py:13
  477.9 61.3 %all-reduce.5.cloned.1.call-done = bf16[48,2,4,1024]{3,0,2,1:T(8,128)(2,1)} async-done(((bf16[48,2,4,1024]{3,0,2,1:T(8,128)(2,1)}), bf16[48,2,4,1024]{3,0,2,1:T(8,128)(2,1)}) %all-reduce.5.cloned.1.call-update) | async-done | bytes 786448 | tf_op jit(solution)/shard_map/psum | solution.py:13
  539.1 2.9 copy.269
  (65 shorter events, 52.4 us)
Async XLA Ops:
  7.2 12.2 %copy-start = (bf16[1,6,768,128]{3,2,1,0:T(8,128)(2,1)S(1)}, bf16[1,6,768,128]{3,2,1,0:T(8,128)(2,1)}, u32[]{:S(2)}) copy-start(bf16[1,6,768,128]{3,2,1,0:T(8,128)(2,1)} %param.5) | copy-start | bytes 3538948
  50.1 21.1 %all-to-all-start.1 = ((bf16[1,48,96,128]{3,1,0,2:T(8,128)(2,1)}), bf16[1,48,96,128]{3,1,0,2:T(8,128)(2,1)S(1)}, u32[]{:S(2)}, u32[]{:S(2)}) async-start(bf16[1,48,96,128]{3,1,0,2:T(8,128)(2,1)} %copy.226), calls=%async_computation.1 | async-start | bytes 2359296 | tf_op jit(solution)/shard_map/all_to_all | solution.py:65
  85.0 6.4 %copy-start.3 = (bf16[48,2,4,1024]{3,2,1,0:T(4,128)(2,1)S(1)}, bf16[48,2,4,1024]{3,2,1,0:T(4,128)(2,1)}, u32[]{:S(2)}) copy-start(bf16[48,2,4,1024]{3,2,1,0:T(4,128)(2,1)} %param.9) | copy-start | bytes 2359300
  85.0 30.9 %all-to-all-start.2 = ((bf16[1,384,12,128]{3,2,0,1:T(8,128)(2,1)}), bf16[1,384,12,128]{3,2,0,1:T(8,128)(2,1)}, u32[]{:S(2)}, u32[]{:S(2)}) async-start(bf16[1,384,12,128]{3,2,0,1:T(8,128)(2,1)} %copy.229), calls=%async_computation.2 | async-start | bytes 3145728 | tf_op jit(solution)/shard_map/all_to_all | solution.py:77
  204.4 21.6 %all-to-all-start.5 = ((bf16[1,48,96,128]{3,2,0,1:T(8,128)(2,1)}), bf16[1,48,96,128]{3,2,0,1:T(8,128)(2,1)}, u32[]{:S(2)}, u32[]{:S(2)}) async-start(bf16[1,48,96,128]{3,2,0,1:T(8,128)(2,1)} %copy.241), calls=%async_computation.5 | async-start | bytes 2359296 | tf_op jit(solution)/shard_map/all_to_all | solution.py:86
  291.1 23.0 %all-to-all-start.8 = ((bf16[1,384,12,128]{3,2,0,1:T(8,128)(2,1)}), bf16[1,384,12,128]{3,2,0,1:T(8,128)(2,1)S(1)}, u32[]{:S(2)}, u32[]{:S(2)}) async-start(bf16[1,384,12,128]{3,2,0,1:T(8,128)(2,1)} %copy.250), calls=%async_computation.8 | async-start | bytes 3145728 | tf_op jit(solution)/shard_map/all_to_all | solution.py:77
  375.2 31.8 %all-to-all-start.10 = ((bf16[1,384,12,128]{3,2,0,1:T(8,128)(2,1)}), bf16[1,384,12,128]{3,2,0,1:T(8,128)(2,1)S(1)}, u32[]{:S(2)}, u32[]{:S(2)}) async-start(bf16[1,384,12,128]{3,2,0,1:T(8,128)(2,1)} %copy.259), calls=%async_computation.10 | async-start | bytes 3145728 | tf_op jit(solution)/shard_map/all_to_all | solution.py:87
  380.3 97.0 %all-reduce.3.cloned.1.call-start = ((), (), s32[]{:S(2)}) async-start(), calls=%async_computation.12 | async-start | bytes 1572864 | tf_op jit(solution)/shard_map/psum | solution.py:13
  408.7 68.7 %copy-start.2 = (bf16[384,2,768]{2,1,0:T(2,128)(2,1)S(1)}, bf16[384,2,768]{2,1,0:T(2,128)(2,1)}, u32[]{:S(2)}) copy-start(bf16[384,2,768]{2,1,0:T(2,128)(2,1)} %copy.215) | copy-start | bytes 3538948
  408.7 133.3 %all-to-all-start.11 = ((bf16[1,48,96,128]{3,2,0,1:T(8,128)(2,1)}), bf16[1,48,96,128]{3,2,0,1:T(8,128)(2,1)S(1)}, u32[]{:S(2)}, u32[]{:S(2)}) async-start(bf16[1,48,96,128]{3,2,0,1:T(8,128)(2,1)} %copy.262), calls=%async_computation.11 | async-start | bytes 2359296 | tf_op jit(solution)/shard_map/all_to_all | solution.py:86
  412.4 126.7 %all-reduce.5.cloned.1.call-start = ((), (), s32[]{:S(2)}) async-start(), calls=%async_computation.13 | async-start | bytes 1572864 | tf_op jit(solution)/shard_map/psum | solution.py:13
  542.0 1.3 copy-start.4
  543.3 2.2 copy-start.1
Sparse Core Ops, SparseCore 0:
  407.0 70.2 all-reduce.2
  480.2 58.8 all-reduce.4
